TPU v7x, 32 devices: a whole 2x2x4 slice. The times are simulated.
32 devices in a mesh: groups: 2 (over y), dp: 4 (over z), tensor: 4 (over x, core).
Axes of the slice: x: 2, y: 2, z: 4, core: 2. Of those that a mesh axis runs over, the one named last changes fastest.
Arguments:
- inputs: bfloat16 [2048, 8192], P(('groups', 'dp'), 'tensor'), parts along dimension 0, may hold values from -6 to 6
- cotangent: bfloat16 [2048, 8192], P(('groups', 'dp'), 'tensor'), parts along dimension 0, may hold values from -6 to 6
- up_blocks: bfloat16 [256, 64, 3, 256], P('dp', 'tensor'), may hold values from -0.21875 to 0.21875
- down_blocks: bfloat16 [256, 64, 3, 256], P('dp', 'tensor'), may hold values from -0.15625 to 0.15625
- low_left: bfloat16 [128, 8192], P(None, 'tensor'), may hold values from -0.0625 to 0.0625
- low_right: bfloat16 [128, 16384], P(None, 'tensor'), may hold values from -0.5 to 0.5
- up_pattern: int32 [64, 3], P('tensor'), may hold values from 0 to 7
- down_pattern: int32 [64, 3], P('tensor'), may hold values from 0 to 7
Outputs:
- grad_input: bfloat16 [2048, 8192], P(('groups', 'dp'), 'tensor'), parts along dimension 0
- grad_up: float32 [512, 64, 3, 256], P(('groups', 'dp'), 'tensor'), parts along dimension 0
- grad_down: float32 [512, 64, 3, 256], P(('groups', 'dp'), 'tensor'), parts along dimension 0
- grad_left: float32 [256, 8192], P(('groups', 'dp'), 'tensor'), parts along dimension 0
- grad_right: float32 [256, 16384], P(('groups', 'dp'), 'tensor'), parts along dimension 0
There are 2 independent parts, one for each index of `groups`. A program takes and returns all parts, laid end to end along the dimension named above; an argument that names none is the same for every part. Nothing has to cross between parts.
Inputs may be any that keep to these rules, and one draw needn't show every extreme that they name: `up_pattern`: feature block within a slice of 8 blocks. `down_pattern`: feature block within a slice of 8 blocks.
All inputs are finite; a program needn't handle non-finite values.
Results may differ from a plain program's by a relative error of at most 0.02.
Values may be sent and summed in bfloat16 or wider, within the bound.
No kernel may reach another device: no remote copies, remote signals or barrier semaphores. Data moves between devices by JAX's collectives and lax.ppermute only.
A program may use at most 128 MiB of HBM per device.

v0:
```python
import math
import jax
import jax.numpy as jnp
from jax import lax
from jax.sharding import PartitionSpec as P

root_coef = 0.7978845608028654
cubic_coef = 0.044715


def swapped(block, axis, distance):
    count = lax.axis_size(axis)
    route = []
    for low in range(count):
        high = low | 1 << distance
        if high != low and high < count:
            route += [(low, high), (high, low)]
    return lax.ppermute(block, axis, route)


def gelu_pair(values):
    inner_arg = root_coef * (values + cubic_coef * values * values * values)
    tangent = jnp.tanh(inner_arg)
    forward = 0.5 * values * (1.0 + tangent)
    slopes = 0.5 * (1.0 + tangent) + 0.5 * values * (1.0 - tangent * tangent) * root_coef * (
        1.0 + 3.0 * cubic_coef * values * values
    )
    return (forward, slopes)


def pick_blocks(slices, pattern, block_size):
    picked = []
    for which_section, source in enumerate(slices):
        shaped = source.reshape(source.shape[0], -1, block_size)
        picked.append(jnp.take(shaped, pattern[:, which_section], axis=1))
    return jnp.stack(picked, axis=2)


def shards(
    inputs, cotangent, up_blocks, down_blocks, low_left, low_right, up_pattern, down_pattern
):
    tokens_here, width_here = inputs.shape
    block_size = up_blocks.shape[3]
    hidden_here = up_blocks.shape[1]
    section_count = up_blocks.shape[2]
    blocks_here = width_here // block_size
    dp_size = lax.axis_size("dp")
    inv_root = 1.0 / math.sqrt(tokens_here * dp_size)
    up_full, down_full = (
        lax.all_gather(up_blocks, "dp", axis=0, tiled=True),
        lax.all_gather(down_blocks, "dp", axis=0, tiled=True),
    )
    sources = [inputs] + [
        swapped(inputs, "tensor", level_bit) for level_bit in range(section_count - 1)
    ]
    selected = pick_blocks(sources, up_pattern, block_size)
    sparse = jnp.einsum("thsi,ihsj->thj", selected, up_full, preferred_element_type=jnp.float32)
    low_part = lax.dot_general(
        inputs, low_left, (((1,), (1,)), ((), ())), preferred_element_type=jnp.float32
    )
    low_sum = lax.psum(low_part.astype(jnp.bfloat16), "tensor")
    preact = sparse.reshape(tokens_here, -1) + jnp.dot(
        low_sum, low_right, preferred_element_type=jnp.float32
    )
    activated, slopes = gelu_pair(preact)
    hidden = activated.astype(jnp.bfloat16)
    picked = pick_blocks([cotangent] * section_count, down_pattern, block_size)
    grad_hidden = jnp.einsum(
        "thso,jhso->thj", picked, down_full, preferred_element_type=jnp.float32
    ).reshape(tokens_here, -1)
    grad_pre = (grad_hidden * slopes).astype(jnp.bfloat16)
    grad_blocks = grad_pre.reshape(tokens_here, hidden_here, block_size)
    slot_ids = jnp.arange(blocks_here, dtype=jnp.int32)

    def section_term(which_section):
        spread = jnp.einsum(
            "thj,ihj->thi",
            grad_blocks,
            up_full[:, :, which_section, :],
            preferred_element_type=jnp.float32,
        )
        placing = (up_pattern[:, which_section][:, None] == slot_ids[None, :]).astype(jnp.float32)
        return jnp.einsum("thi,hd->tdi", spread, placing).reshape(tokens_here, width_here)

    own_term = section_term(0)
    for level_bit in range(section_count - 1):
        outgoing = section_term(level_bit + 1).astype(jnp.bfloat16)
        own_term = own_term + swapped(outgoing, "tensor", level_bit).astype(jnp.float32)
    back_part = lax.dot_general(
        grad_pre, low_right, (((1,), (1,)), ((), ())), preferred_element_type=jnp.float32
    )
    back_low = lax.psum(back_part.astype(jnp.bfloat16), "tensor")
    grad_input = (
        own_term + jnp.dot(back_low, low_left, preferred_element_type=jnp.float32)
    ).astype(jnp.bfloat16)
    row_part = selected
    grad_up = lax.psum_scatter(
        (
            jnp.einsum("thsi,thj->ihsj", row_part, grad_blocks, preferred_element_type=jnp.float32)
            * inv_root
        ).astype(jnp.bfloat16),
        "dp",
        scatter_dimension=0,
        tiled=True,
    ).astype(jnp.float32)
    hidden_blocks = hidden.reshape(tokens_here, hidden_here, block_size)
    row_part = hidden_blocks
    grad_down = lax.psum_scatter(
        (
            jnp.einsum("thj,thso->jhso", row_part, picked, preferred_element_type=jnp.float32)
            * inv_root
        ).astype(jnp.bfloat16),
        "dp",
        scatter_dimension=0,
        tiled=True,
    ).astype(jnp.float32)
    row_part = back_low
    grad_left = lax.psum_scatter(
        (
            lax.dot_general(
                row_part, inputs, (((0,), (0,)), ((), ())), preferred_element_type=jnp.float32
            )
            * inv_root
        ).astype(jnp.bfloat16),
        "dp",
        scatter_dimension=0,
        tiled=True,
    ).astype(jnp.float32)
    row_part = low_sum
    grad_right = lax.psum_scatter(
        (
            lax.dot_general(
                row_part, grad_pre, (((0,), (0,)), ((), ())), preferred_element_type=jnp.float32
            )
            * inv_root
        ).astype(jnp.bfloat16),
        "dp",
        scatter_dimension=0,
        tiled=True,
    ).astype(jnp.float32)
    return (grad_input, grad_up, grad_down, grad_left, grad_right)


def solution(mesh):
    in_specs = (
        P(("groups", "dp"), "tensor"),
        P(("groups", "dp"), "tensor"),
        P("dp", "tensor", None, None),
        P("dp", "tensor", None, None),
        P(None, "tensor"),
        P(None, "tensor"),
        P("tensor", None),
        P("tensor", None),
    )
    out_specs = (
        P(("groups", "dp"), "tensor"),
        P(("groups", "dp"), "tensor", None, None),
        P(("groups", "dp"), "tensor", None, None),
        P(("groups", "dp"), "tensor"),
        P(("groups", "dp"), "tensor"),
    )
    return jax.shard_map(shards, mesh=mesh, in_specs=in_specs, out_specs=out_specs, check_vma=False)
```

profile of v0, /device:TPU:0, one launch (start us, length us, event | category | flops | bytes accessed | tf_op | source)
XLA Modules:
  0.0 590.4 jit_solution(4953019336405703996)
XLA Ops:
  8.1 3.2 copy.60
  11.3 3.2 copy.67
  14.6 0.0 all-reduce.3.cloned.1.call-start
  14.6 0.5 copy.61
  15.2 3.0 collective-permute-start.1
  18.2 2.1 convolution_convert_fusion.1
  20.4 2.3 copy.56
  22.7 1.5 copy.57
  24.3 2.0 gather_fusion.2
  26.3 2.0 gather_fusion.1
  28.3 2.1 gather_fusion
  30.4 0.5 copy.62
  30.9 2.0 gather_fusion.3
  32.9 3.4 select_bitcast_fusion.5
  36.3 1.6 select_bitcast_fusion.2
  37.9 0.7 copy-done.3
  38.7 0.7 copy-done.4
  39.3 2.4 select_bitcast_fusion.3
  41.8 0.2 collective-permute-done.1
  42.0 1.5 copy.66
  43.5 1.5 copy.64
  45.0 2.0 gather_fusion.5
  47.0 2.1 gather_fusion.4
  49.1 4.8 select_bitcast_fusion
  53.9 75.6 %all-gather.3.cloned.1.call-done = bf16[256,16,3,256]{3,0,2,1:T(8,128)(2,1)} async-done(((bf16[64,16,3,256]{3,0,2,1:T(8,128)(2,1)}), bf16[256,16,3,256]{3,0,2,1:T(8,128)(2,1)}) %all-gather.3.cloned.1.call-update) | async-done | bytes 6291472 | tf_op jit(solution)/shard_map/all_gather | solution.py:51
  129.5 7.9 %fusion.17 = f32[16,256,256,1]{1,2,3,0:T(8,128)} fusion(bf16[256,16,3,256]{3,0,2,1:T(8,128)(2,1)} %all-gather.3.cloned.1.call-done, bf16[256,16,1,256]{3,0,2,1:T(8,128)(2,1)S(1)} %copy-done.6, bf16[256,16,1,256]{3,0,2,1:T(8,128)(2,1)} %get-tuple-element.47, bf16[256,16,1,256]{3,0,2,1:T(8,128)(2,1)} %select_bitcast_fusion.5), kind=kOutput, calls=%fused_computation.32 | convolution fusion | flops 1616904192 | bytes 16777216 | tf_op jit(solution)/shard_map/thso,jhso->thj/dot_general | solution.py:68
  137.3 107.2 %all-gather.5.cloned.1.call-done = bf16[256,16,3,256]{3,0,2,1:T(8,128)(2,1)} async-done(((bf16[64,16,3,256]{3,0,2,1:T(8,128)(2,1)}), bf16[256,16,3,256]{3,0,2,1:T(8,128)(2,1)}) %all-gather.5.cloned.1.call-update) | async-done | bytes 6291472 | tf_op jit(solution)/shard_map/all_gather | solution.py:50
  244.6 8.8 %fusion.16 = f32[16,256,256,1]{1,2,3,0:T(8,128)} fusion(bf16[256,16,3,256]{3,0,2,1:T(8,128)(2,1)} %all-gather.5.cloned.1.call-done, bf16[256,16,1,256]{3,0,2,1:T(8,128)(2,1)} %get-tuple-element.48, bf16[256,16,1,256]{3,0,2,1:T(8,128)(2,1)} %get-tuple-element.49, bf16[256,16,1,256]{3,0,2,1:T(8,128)(2,1)} %select_bitcast_fusion.2), kind=kOutput, calls=%fused_computation.31 | convolution fusion | flops 1616904192 | bytes 16777216 | tf_op jit(solution)/shard_map/thsi,ihsj->thj/dot_general | solution.py:57
  253.4 5.7 copy.69
  259.1 5.7 copy.68
  264.8 6.7 %multiply_convert_fusion.2 = (bf16[256,4096]{1,0:T(8,128)(2,1)}, bf16[256,4096]{1,0:T(8,128)(2,1)S(1)}) fusion(f32[256,4096]{1,0:T(8,128)} %copy.69, f32[256,4096]{1,0:T(8,128)} %copy.68, bf16[256,128]{1,0:T(8,128)(2,1)} %all-reduce.3.cloned.1.call-done, bf16[128,4096]{1,0:T(8,128)(2,1)S(1)} %copy-done), kind=kOutput, calls=%fused_computation.30 | convolution fusion | flops 291504128 | bytes 13697024 | tf_op jit(solution)/shard_map/dot_general | solution.py:62
  271.5 1.3 convolution_convert_fusion
  272.9 29.5 %all-reduce.5.cloned.1.call-done = bf16[256,128]{1,0:T(8,128)(2,1)} async-done(((bf16[256,128]{1,0:T(8,128)(2,1)}), bf16[256,128]{1,0:T(8,128)(2,1)}) %all-reduce.5.cloned.1.call-update) | async-done | bytes 65552 | tf_op jit(solution)/shard_map/psum | solution.py:92
  302.4 2.4 fusion.18
  304.9 1.5 fusion.2
  306.4 0.2 reduce-scatter.5.cloned.1.call-start
  306.7 0.6 copy.94
  307.3 0.9 copy-done.9
  308.2 0.6 copy-done.10
  308.9 6.3 %fusion = bf16[256,16,3,256]{0,3,2,1:T(8,128)(2,1)} fusion(bf16[256,16,1,256]{3,0,2,1:T(8,128)(2,1)S(1)} %copy-done.9, bf16[256,16,1,256]{3,0,2,1:T(8,128)(2,1)S(1)} %copy-done.10, bf16[256,16,1,256]{3,0,2,1:T(8,128)(2,1)} %select_bitcast_fusion.2, bf16[256,16,256,1]{2,1,0,3:T(8,128)(2,1)S(1)} %bitcast.145), kind=kOutput, calls=%fused_computation.8 | convolution fusion | flops 1635778560 | bytes 14680064 | tf_op jit(solution)/shard_map/thsi,thj->ihsj/dot_general | solution.py:99
  315.2 9.1 %copy.77 = bf16[256,16,3,256]{3,1,2,0:T(8,128)(2,1)} copy(bf16[256,16,3,256]{0,3,2,1:T(8,128)(2,1)} %fusion) | data formatting | bytes 12582912 | tf_op jit(solution)/shard_map/convert_element_type | solution.py:101
  324.3 2.4 copy.95
  326.7 0.5 copy-done.8
  327.2 6.8 %fusion.1 = bf16[256,16,3,256]{0,3,2,1:T(8,128)(2,1)} fusion(bf16[256,16,1,256]{3,0,2,1:T(8,128)(2,1)S(1)} %copy-done.7, bf16[256,16,1,256]{3,0,2,1:T(8,128)(2,1)S(1)} %copy-done.8, bf16[256,16,1,256]{3,0,2,1:T(8,128)(2,1)} %select_bitcast_fusion.5, bf16[256,16,256,1]{2,1,0,3:T(8,128)(2,1)S(1)} %bitcast.144), kind=kOutput, calls=%fused_computation.9 | convolution fusion | flops 1623195648 | bytes 14680064 | tf_op jit(solution)/shard_map/thj,thso->jhso/dot_general | solution.py:110
  334.0 8.9 %copy.80 = bf16[256,16,3,256]{3,1,2,0:T(8,128)(2,1)} copy(bf16[256,16,3,256]{0,3,2,1:T(8,128)(2,1)} %fusion.1) | data formatting | bytes 12582912 | tf_op jit(solution)/shard_map/convert_element_type | solution.py:112
  343.0 2.4 convolution_bitcast_fusion
  345.4 1.3 fusion.30
  346.7 0.3 copy.93
  347.0 0.2 collective-permute-start.3
  347.2 2.3 convolution_bitcast_fusion.1
  349.5 1.3 fusion.27
  350.8 0.3 copy.92
  351.1 0.1 collective-permute-start.2
  351.2 2.4 convolution_bitcast_fusion.2
  353.6 1.3 fusion.14
  354.8 0.9 copy.91
  355.7 14.6 %collective-permute-done.3 = bf16[256,2048]{1,0:T(8,128)(2,1)S(1)} collective-permute-done((bf16[256,2048]{1,0:T(8,128)(2,1)S(1)}, bf16[256,2048]{1,0:T(8,128)(2,1)S(1)}, u32[]{:S(2)}, u32[]{:S(2)}) %collective-permute-start.3) | collective-permute-done | bytes 1048608 | tf_op jit(solution)/shard_map/ppermute | solution.py:18
  370.3 1.5 add_convert_fusion
  371.9 1.6 convert_element_type.92
  373.5 1.8 convert_element_type.94
  375.3 90.7 %reduce-scatter.5.cloned.1.call-done = bf16[64,16,3,256]{3,1,2,0:T(8,128)(2,1)} async-done(((bf16[256,16,3,256]{3,1,2,0:T(8,128)(2,1)}), bf16[64,16,3,256]{3,1,2,0:T(8,128)(2,1)}) %reduce-scatter.5.cloned.1.call-update) | async-done | bytes 1572880 | tf_op jit(solution)/shard_map/reduce_scatter | solution.py:97
  466.0 3.6 convert_element_type.86
  469.6 109.9 %reduce-scatter.7.cloned.1.call-done = bf16[64,16,3,256]{3,1,2,0:T(8,128)(2,1)} async-done(((bf16[256,16,3,256]{3,1,2,0:T(8,128)(2,1)}), bf16[64,16,3,256]{3,1,2,0:T(8,128)(2,1)}) %reduce-scatter.7.cloned.1.call-update) | async-done | bytes 1572880 | tf_op jit(solution)/shard_map/reduce_scatter | solution.py:108
  579.5 3.5 convert_element_type.90
  (56 shorter events, 0.5 us)
Async XLA Ops:
  8.0 256.8 %copy-start = (bf16[128,4096]{1,0:T(8,128)(2,1)S(1)}, bf16[128,4096]{1,0:T(8,128)(2,1)}, u32[]{:S(2)}) copy-start(bf16[128,4096]{1,0:T(8,128)(2,1)} %param.15) | copy-start | bytes 3145732
  8.0 121.5 %all-gather.3.cloned.1.call-start = ((), (), s32[]{:S(2)}) async-start(), calls=%async_computation.4 | async-start | bytes 7864320 | tf_op jit(solution)/shard_map/all_gather | solution.py:51
  11.3 3.3 copy-start.2
  11.3 233.3 %all-gather.5.cloned.1.call-start = ((), (), s32[]{:S(2)}) async-start(), calls=%async_computation.5 | async-start | bytes 7864320 | tf_op jit(solution)/shard_map/all_gather | solution.py:50
  14.6 250.2 %all-reduce.3.cloned.1.call-start = ((), (), s32[]{:S(2)}) async-start(), calls=%async_computation.6 | async-start | bytes 131072 | tf_op jit(solution)/shard_map/psum | solution.py:61
  15.2 26.8 %collective-permute-start.1 = (bf16[256,2048]{0,1:T(8,128)(2,1)S(1)}, bf16[256,2048]{0,1:T(8,128)(2,1)}, u32[]{:S(2)}, u32[]{:S(2)}) collective-permute-start(bf16[256,2048]{0,1:T(8,128)(2,1)S(1)} %copy.61), channel_id=1, source_target_pairs={{0,2},{2,0},{1,3},{3,1},{4,6},{6,4},{5,7},{7,5},{8,10},{10,8},{9,1... | collective-permute-start | bytes 3145736 | tf_op jit(solution)/shard_map/ppermute | solution.py:18
  18.2 25.3 %collective-permute-start = (bf16[256,2048]{0,1:T(8,128)(2,1)S(1)}, bf16[256,2048]{0,1:T(8,128)(2,1)}, u32[]{:S(2)}, u32[]{:S(2)}) collective-permute-start(bf16[256,2048]{0,1:T(8,128)(2,1)S(1)} %copy.61), channel_id=1, source_target_pairs={{0,1},{1,0},{2,3},{3,2},{4,5},{5,4},{6,7},{7,6},{8,9},{9,8},{10,11... | collective-permute-start | bytes 3145736 | tf_op jit(solution)/shard_map/ppermute | solution.py:18
  20.3 3.9 copy-start.15
  20.3 282.1 %all-reduce.5.cloned.1.call-start = ((), (), s32[]{:S(2)}) async-start(), calls=%async_computation.7 | async-start | bytes 131072 | tf_op jit(solution)/shard_map/psum | solution.py:92
  28.3 2.1 copy-start.14
  32.9 3.4 copy-start.5
  36.3 2.4 copy-start.3
  36.3 3.0 copy-start.4
  49.1 80.4 %copy-start.6 = (bf16[256,16,1,256]{3,0,2,1:T(8,128)(2,1)S(1)}, bf16[256,16,1,256]{3,0,2,1:T(8,128)(2,1)}, u32[]{:S(2)}) copy-start(bf16[256,16,1,256]{3,0,2,1:T(8,128)(2,1)} %get-tuple-element.46) | copy-start | bytes 6291460
  271.5 33.4 %copy-start.13 = (bf16[256,128]{1,0:T(8,128)(2,1)S(1)}, bf16[256,128]{1,0:T(8,128)(2,1)}, u32[]{:S(2)}) copy-start(bf16[256,128]{1,0:T(8,128)(2,1)} %all-reduce.3.cloned.1.call-done) | copy-start | bytes 196612
  272.8 99.0 %reduce-scatter.9.cloned.1.call-start = ((), (), s32[]{:S(2)}) async-start(), calls=%async_computation.10 | async-start | bytes 655360 | tf_op jit(solution)/shard_map/reduce_scatter | solution.py:118
  304.8 68.7 %reduce-scatter.11.cloned.1.call-start = ((), (), s32[]{:S(2)}) async-start(), calls=%async_computation.11 | async-start | bytes 1310720 | tf_op jit(solution)/shard_map/reduce_scatter | solution.py:130
  306.4 159.6 %reduce-scatter.5.cloned.1.call-start = ((), (), s32[]{:S(2)}) async-start(), calls=%async_computation.8 | async-start | bytes 7864320 | tf_op jit(solution)/shard_map/reduce_scatter | solution.py:97
  306.6 1.6 copy-start.9
  306.6 2.2 copy-start.10
  324.2 255.2 %reduce-scatter.7.cloned.1.call-start = ((), (), s32[]{:S(2)}) async-start(), calls=%async_computation.9 | async-start | bytes 7864320 | tf_op jit(solution)/shard_map/reduce_scatter | solution.py:108
  324.3 2.4 copy-start.7
  324.3 2.9 copy-start.8
  347.0 23.4 %collective-permute-start.3 = (bf16[256,2048]{1,0:T(8,128)(2,1)S(1)}, bf16[256,2048]{1,0:T(8,128)(2,1)S(1)}, u32[]{:S(2)}, u32[]{:S(2)}) collective-permute-start(bf16[256,2048]{1,0:T(8,128)(2,1)S(1)} %bitcast.146), channel_id=1, source_target_pairs={{0,2},{2,0},{1,3},{3,1},{4,6},{6,4},{5,7},{7,5},{8,10},{10,8},{9,1... | collective-permute-start | bytes 3145736 | tf_op jit(solution)/shard_map/ppermute | solution.py:18
  351.1 19.2 %collective-permute-start.2 = (bf16[256,2048]{1,0:T(8,128)(2,1)S(1)}, bf16[256,2048]{1,0:T(8,128)(2,1)S(1)}, u32[]{:S(2)}, u32[]{:S(2)}) collective-permute-start(bf16[256,2048]{1,0:T(8,128)(2,1)S(1)} %bitcast.147), channel_id=1, source_target_pairs={{0,1},{1,0},{2,3},{3,2},{4,5},{5,4},{6,7},{7,6},{8,9},{9,8},{10,11... | collective-permute-start | bytes 3145736 | tf_op jit(solution)/shard_map/ppermute | solution.py:18
  354.8 15.5 %copy-start.11 = (bf16[128,2048]{1,0:T(8,128)(2,1)S(1)}, bf16[128,2048]{1,0:T(8,128)(2,1)}, u32[]{:S(2)}) copy-start(bf16[128,2048]{1,0:T(8,128)(2,1)} %param.14) | copy-start | bytes 1572868
  354.8 15.5 %copy-start.12 = (bf16[256,128]{1,0:T(8,128)(2,1)S(1)}, bf16[256,128]{1,0:T(8,128)(2,1)}, u32[]{:S(2)}) copy-start(bf16[256,128]{1,0:T(8,128)(2,1)} %all-reduce.5.cloned.1.call-done) | copy-start | bytes 196612
  466.0 117.0 %copy-start.1 = (bf16[128,4096]{1,0:T(8,128)(2,1)S(1)}, bf16[128,4096]{1,0:T(8,128)(2,1)}, u32[]{:S(2)}) copy-start(bf16[128,4096]{1,0:T(8,128)(2,1)} %param.15) | copy-start | bytes 3145732
Sparse Core Ops, SparseCore 0:
  11.4 118.0 all-gather.2
  131.0 113.4 all-gather.4
  305.0 21.8 reduce-scatter.8
  329.0 25.5 reduce-scatter.10
  356.7 109.2 reduce-scatter.4
  468.2 111.2 reduce-scatter.6
Sparse Core Ops, SparseCore 1:
  20.4 31.8 all-reduce.2
  272.9 29.4 all-reduce.4
where the time goes:
time: 592 us; the launch traced here: 590 us
  waiting for transfers between devices  428 us (72%)
  local copies, waits for them, and re-layouts  63.8 us (11%)
  matrix products  56.2 us (9%)
  other arithmetic  22.9 us (4%)
  between operations  15.9 us (3%)
    reduce_scatter x1, waiting for transfers between devices, shards(): lax.psum_scatter((jnp.einsum('thj,thso->jhso', row_part, picked, preferre...  110 us
    all_gather x1, waiting for transfers between devices, shards(): lax.all_gather(up_blocks, 'dp', axis=0, tiled=True)  107 us
    reduce_scatter x1, waiting for transfers between devices, shards(): lax.psum_scatter((jnp.einsum('thsi,thj->ihsj', row_part, grad_blocks, pre...  90.7 us
    all_gather x1, waiting for transfers between devices, shards(): lax.all_gather(down_blocks, 'dp', axis=0, tiled=True)  75.6 us
    psum x1, waiting for transfers between devices, shards(): back_low = lax.psum(back_part.astype(jnp.bfloat16), 'tensor')  29.5 us
    unnamed x41, local copies, waits for them, and re-layouts  17.2 us
    ppermute x4, waiting for transfers between devices, swapped(): return lax.ppermute(block, axis, route)  14.8 us
    another operation x4, other arithmetic, pick_blocks(): return jnp.stack(picked, axis=2)  12.3 us
  transfers between devices with their start and end apart: 12, of which 7 were waited for; matrix products, arithmetic and copies ran while one was open for 21% of the time, Pallas kernels for 0%

commit v1 on v0

--- a/solution.py
+++ b/solution.py
@@ -89,7 +89,8 @@
     back_part = lax.dot_general(
         grad_pre, low_right, (((1,), (1,)), ((), ())), preferred_element_type=jnp.float32
     )
-    back_low = lax.psum(back_part.astype(jnp.bfloat16), "tensor")
+    x_local = back_part.astype(jnp.bfloat16)
+    back_low = jax.lax.all_gather(x_local, axis_name="tensor").sum(axis=0)
     grad_input = (
         own_term + jnp.dot(back_low, low_left, preferred_element_type=jnp.float32)
     ).astype(jnp.bfloat16)

time: 592 us -> 566 us (0.956)
  waiting for transfers between devices: 428 us -> 392 us
    psum x1 -> x0, waiting for transfers between devices: 29.5 us -> none  [shards(): back_low = lax.psum(back_part.astype(jnp.bfloat16), 'tensor')]
    unnamed x41 -> x39, local copies, waits for them, and re-layouts: 17.2 us -> 19.2 us
  transfers between devices with their start and end apart: 12 -> 11, of which waited for: 7 -> 6; matrix products, arithmetic and copies ran while one was open for 21% -> 22% of each run, Pallas kernels for 0% -> 0%
where the time goes in v1:
time: 566 us; the launch traced here: 564 us
  waiting for transfers between devices  392 us (69%)
  local copies, waits for them, and re-layouts  65.6 us (12%)
  matrix products  57 us (10%)
  other arithmetic  23 us (4%)
  between operations  15.9 us (3%)
  blocking collectives  5.91 us (1%)
    reduce_scatter x1, waiting for transfers between devices, shards(): lax.psum_scatter((jnp.einsum('thj,thso->jhso', row_part, picked, preferre...  110 us
    all_gather x1, waiting for transfers between devices, shards(): lax.all_gather(up_blocks, 'dp', axis=0, tiled=True)  107 us
    reduce_scatter x1, waiting for transfers between devices, shards(): lax.psum_scatter((jnp.einsum('thsi,thj->ihsj', row_part, grad_blocks, pre...  85.8 us
    all_gather x1, waiting for transfers between devices, shards(): lax.all_gather(down_blocks, 'dp', axis=0, tiled=True)  75.5 us
    unnamed x39, local copies, waits for them, and re-layouts  19.2 us
    ppermute x4, waiting for transfers between devices, swapped(): return lax.ppermute(block, axis, route)  13.3 us
    another operation x4, other arithmetic, pick_blocks(): return jnp.stack(picked, axis=2)  12.3 us
    gather x6, local copies, waits for them, and re-layouts, pick_blocks(): picked.append(jnp.take(shaped, pattern[:, which_section], axis=1))  12.2 us
  transfers between devices with their start and end apart: 11, of which 6 were waited for; matrix products, arithmetic and copies ran while one was open for 22% of the time, Pallas kernels for 0%

profile of v1, /device:TPU:0, one launch (start us, length us, event | category | flops | bytes accessed | tf_op | source)
XLA Modules:
  0.0 564.3 jit_solution(13817751218234281229)
XLA Ops:
  8.1 3.2 copy.60
  11.4 3.2 copy.67
  14.6 0.0 all-reduce.2.cloned.1.call-start
  14.6 0.5 copy.61
  15.2 3.0 collective-permute-start.1
  18.2 2.1 convolution_convert_fusion.1
  20.4 2.3 copy.56
  22.7 1.5 copy.57
  24.3 2.0 gather_fusion.2
  26.3 2.0 gather_fusion.1
  28.3 2.1 gather_fusion
  30.4 0.5 copy.62
  31.0 2.0 gather_fusion.3
  33.0 3.4 select_bitcast_fusion.5
  36.4 1.6 select_bitcast_fusion.2
  38.0 0.7 copy-done.3
  38.7 0.7 copy-done.4
  39.4 2.4 select_bitcast_fusion.3
  41.8 0.2 collective-permute-done.1
  42.0 1.5 copy.66
  43.5 1.5 copy.64
  45.0 2.0 gather_fusion.5
  47.0 2.1 gather_fusion.4
  49.1 4.9 select_bitcast_fusion
  53.9 75.5 %all-gather.4.cloned.1.call-done = bf16[256,16,3,256]{3,0,2,1:T(8,128)(2,1)} async-done(((bf16[64,16,3,256]{3,0,2,1:T(8,128)(2,1)}), bf16[256,16,3,256]{3,0,2,1:T(8,128)(2,1)}) %all-gather.4.cloned.1.call-update) | async-done | bytes 6291472 | tf_op jit(solution)/shard_map/all_gather | solution.py:51
  129.5 7.9 %fusion.17 = f32[16,256,256,1]{1,2,3,0:T(8,128)} fusion(bf16[256,16,3,256]{3,0,2,1:T(8,128)(2,1)} %all-gather.4.cloned.1.call-done, bf16[256,16,1,256]{3,0,2,1:T(8,128)(2,1)S(1)} %copy-done.6, bf16[256,16,1,256]{3,0,2,1:T(8,128)(2,1)} %get-tuple-element.47, bf16[256,16,1,256]{3,0,2,1:T(8,128)(2,1)} %select_bitcast_fusion.5), kind=kOutput, calls=%fused_computation.32 | convolution fusion | flops 1616904192 | bytes 16777216 | tf_op jit(solution)/shard_map/thso,jhso->thj/dot_general | solution.py:68
  137.4 107.3 %all-gather.6.cloned.1.call-done = bf16[256,16,3,256]{3,0,2,1:T(8,128)(2,1)} async-done(((bf16[64,16,3,256]{3,0,2,1:T(8,128)(2,1)}), bf16[256,16,3,256]{3,0,2,1:T(8,128)(2,1)}) %all-gather.6.cloned.1.call-update) | async-done | bytes 6291472 | tf_op jit(solution)/shard_map/all_gather | solution.py:50
  244.6 8.8 %fusion.16 = f32[16,256,256,1]{1,2,3,0:T(8,128)} fusion(bf16[256,16,3,256]{3,0,2,1:T(8,128)(2,1)} %all-gather.6.cloned.1.call-done, bf16[256,16,1,256]{3,0,2,1:T(8,128)(2,1)} %get-tuple-element.48, bf16[256,16,1,256]{3,0,2,1:T(8,128)(2,1)} %get-tuple-element.49, bf16[256,16,1,256]{3,0,2,1:T(8,128)(2,1)} %select_bitcast_fusion.2), kind=kOutput, calls=%fused_computation.31 | convolution fusion | flops 1616904192 | bytes 16777216 | tf_op jit(solution)/shard_map/thsi,ihsj->thj/dot_general | solution.py:57
  253.4 5.7 %copy.69 = f32[256,4096]{1,0:T(8,128)} copy(f32[256,4096]{0,1:T(8,128)} %bitcast.138) | data formatting | bytes 8388608 | tf_op jit(solution)/shard_map/reshape | solution.py:70
  259.1 5.6 %copy.68 = f32[256,4096]{1,0:T(8,128)} copy(f32[256,4096]{0,1:T(8,128)} %bitcast.139) | data formatting | bytes 8388608 | tf_op jit(solution)/shard_map/reshape | solution.py:62
  264.7 6.7 %multiply_convert_fusion.2 = (bf16[256,4096]{1,0:T(8,128)(2,1)}, bf16[256,4096]{1,0:T(8,128)(2,1)S(1)}) fusion(f32[256,4096]{1,0:T(8,128)} %copy.69, f32[256,4096]{1,0:T(8,128)} %copy.68, bf16[256,128]{1,0:T(8,128)(2,1)} %all-reduce.2.cloned.1.call-done, bf16[128,4096]{1,0:T(8,128)(2,1)S(1)} %copy-done), kind=kOutput, calls=%fused_computation.30 | convolution fusion | flops 291504128 | bytes 13697024 | tf_op jit(solution)/shard_map/dot_general | solution.py:62
  271.4 0.7 convolution_convert_fusion
  272.1 5.9 %all-gather = bf16[1024,128]{1,0:T(8,128)(2,1)S(1)} all-gather(bf16[256,128]{1,0:T(8,128)(2,1)S(1)} %convolution_convert_fusion), channel_id=2, replica_groups=mesh['groups'=2,'dp'=4,'tensor'=4] {'tensor'}, dimensions={0}, use_global_device_ids=true | all-gather | bytes 327680 | tf_op jit(solution)/shard_map/all_gather | solution.py:93
  278.1 2.4 fusion.18
  280.5 1.5 fusion.2
  282.1 0.2 reduce-scatter.5.cloned.1.call-start
  282.3 0.6 copy.94
  283.0 0.9 copy-done.9
  283.9 0.6 copy-done.10
  284.5 6.3 %fusion = bf16[256,16,3,256]{0,3,2,1:T(8,128)(2,1)} fusion(bf16[256,16,1,256]{3,0,2,1:T(8,128)(2,1)S(1)} %copy-done.9, bf16[256,16,1,256]{3,0,2,1:T(8,128)(2,1)S(1)} %copy-done.10, bf16[256,16,1,256]{3,0,2,1:T(8,128)(2,1)} %select_bitcast_fusion.2, bf16[256,16,256,1]{2,1,0,3:T(8,128)(2,1)S(1)} %bitcast.146), kind=kOutput, calls=%fused_computation.8 | convolution fusion | flops 1635778560 | bytes 14680064 | tf_op jit(solution)/shard_map/thsi,thj->ihsj/dot_general | solution.py:100
  290.8 9.0 %copy.77 = bf16[256,16,3,256]{3,1,2,0:T(8,128)(2,1)} copy(bf16[256,16,3,256]{0,3,2,1:T(8,128)(2,1)} %fusion) | data formatting | bytes 12582912 | tf_op jit(solution)/shard_map/convert_element_type | solution.py:102
  299.9 2.4 copy.95
  302.3 0.4 copy-done.8
  302.8 6.8 %fusion.1 = bf16[256,16,3,256]{0,3,2,1:T(8,128)(2,1)} fusion(bf16[256,16,1,256]{3,0,2,1:T(8,128)(2,1)S(1)} %copy-done.7, bf16[256,16,1,256]{3,0,2,1:T(8,128)(2,1)S(1)} %copy-done.8, bf16[256,16,1,256]{3,0,2,1:T(8,128)(2,1)} %select_bitcast_fusion.5, bf16[256,16,256,1]{2,1,0,3:T(8,128)(2,1)S(1)} %bitcast.145), kind=kOutput, calls=%fused_computation.9 | convolution fusion | flops 1623195648 | bytes 14680064 | tf_op jit(solution)/shard_map/thj,thso->jhso/dot_general | solution.py:111
  309.6 8.9 %copy.80 = bf16[256,16,3,256]{3,1,2,0:T(8,128)(2,1)} copy(bf16[256,16,3,256]{0,3,2,1:T(8,128)(2,1)} %fusion.1) | data formatting | bytes 12582912 | tf_op jit(solution)/shard_map/convert_element_type | solution.py:113
  318.6 2.3 convolution_bitcast_fusion
  320.9 1.3 fusion.30
  322.2 1.3 copy.93
  323.5 1.5 collective-permute-start.3
  325.0 2.4 convolution_bitcast_fusion.1
  327.4 1.3 fusion.27
  328.6 1.3 copy.92
  329.9 0.1 collective-permute-start.2
  330.0 2.3 convolution_bitcast_fusion.2
  332.3 1.3 fusion.14
  333.6 0.9 copy.91
  334.5 1.7 convert_element_type.94
  336.2 13.1 %collective-permute-done.3 = bf16[256,2048]{1,0:T(8,128)(2,1)} collective-permute-done((bf16[256,2048]{1,0:T(8,128)(2,1)}, bf16[256,2048]{1,0:T(8,128)(2,1)}, u32[]{:S(2)}, u32[]{:S(2)}) %collective-permute-start.3) | collective-permute-done | bytes 1048608 | tf_op jit(solution)/shard_map/ppermute | solution.py:18
  349.3 3.0 add_convert_fusion
  352.3 1.8 convert_element_type.96
  354.0 85.8 %reduce-scatter.5.cloned.1.call-done = bf16[64,16,3,256]{3,1,2,0:T(8,128)(2,1)} async-done(((bf16[256,16,3,256]{3,1,2,0:T(8,128)(2,1)}), bf16[64,16,3,256]{3,1,2,0:T(8,128)(2,1)}) %reduce-scatter.5.cloned.1.call-update) | async-done | bytes 1572880 | tf_op jit(solution)/shard_map/reduce_scatter | solution.py:98
  439.9 3.6 convert_element_type.88
  443.5 109.9 %reduce-scatter.7.cloned.1.call-done = bf16[64,16,3,256]{3,1,2,0:T(8,128)(2,1)} async-done(((bf16[256,16,3,256]{3,1,2,0:T(8,128)(2,1)}), bf16[64,16,3,256]{3,1,2,0:T(8,128)(2,1)}) %reduce-scatter.7.cloned.1.call-update) | async-done | bytes 1572880 | tf_op jit(solution)/shard_map/reduce_scatter | solution.py:109
  553.3 3.5 convert_element_type.92
  (53 shorter events, 0.5 us)
Async XLA Ops:
  8.0 256.7 %copy-start = (bf16[128,4096]{1,0:T(8,128)(2,1)S(1)}, bf16[128,4096]{1,0:T(8,128)(2,1)}, u32[]{:S(2)}) copy-start(bf16[128,4096]{1,0:T(8,128)(2,1)} %param.15) | copy-start | bytes 3145732
  8.0 121.5 %all-gather.4.cloned.1.call-start = ((), (), s32[]{:S(2)}) async-start(), calls=%async_computation.4 | async-start | bytes 7864320 | tf_op jit(solution)/shard_map/all_gather | solution.py:51
  11.3 3.3 copy-start.2
  11.3 233.3 %all-gather.6.cloned.1.call-start = ((), (), s32[]{:S(2)}) async-start(), calls=%async_computation.5 | async-start | bytes 7864320 | tf_op jit(solution)/shard_map/all_gather | solution.py:50
  14.6 250.1 %all-reduce.2.cloned.1.call-start = ((), (), s32[]{:S(2)}) async-start(), calls=%async_computation.6 | async-start | bytes 131072 | tf_op jit(solution)/shard_map/psum | solution.py:61
  15.2 26.8 %collective-permute-start.1 = (bf16[256,2048]{0,1:T(8,128)(2,1)S(1)}, bf16[256,2048]{0,1:T(8,128)(2,1)}, u32[]{:S(2)}, u32[]{:S(2)}) collective-permute-start(bf16[256,2048]{0,1:T(8,128)(2,1)S(1)} %copy.61), channel_id=1, source_target_pairs={{0,2},{2,0},{1,3},{3,1},{4,6},{6,4},{5,7},{7,5},{8,10},{10,8},{9,1... | collective-permute-start | bytes 3145736 | tf_op jit(solution)/shard_map/ppermute | solution.py:18
  18.2 25.3 %collective-permute-start = (bf16[256,2048]{0,1:T(8,128)(2,1)S(1)}, bf16[256,2048]{0,1:T(8,128)(2,1)}, u32[]{:S(2)}, u32[]{:S(2)}) collective-permute-start(bf16[256,2048]{0,1:T(8,128)(2,1)S(1)} %copy.61), channel_id=1, source_target_pairs={{0,1},{1,0},{2,3},{3,2},{4,5},{5,4},{6,7},{7,6},{8,9},{9,8},{10,11... | collective-permute-start | bytes 3145736 | tf_op jit(solution)/shard_map/ppermute | solution.py:18
  20.3 3.9 copy-start.14
  20.3 314.2 %reduce-scatter.9.cloned.1.call-start = ((), (), s32[]{:S(2)}) async-start(), calls=%async_computation.9 | async-start | bytes 655360 | tf_op jit(solution)/shard_map/reduce_scatter | solution.py:119
  28.3 2.1 copy-start.13
  32.9 3.4 copy-start.5
  36.3 2.4 copy-start.3
  36.4 3.0 copy-start.4
  49.1 80.4 %copy-start.6 = (bf16[256,16,1,256]{3,0,2,1:T(8,128)(2,1)S(1)}, bf16[256,16,1,256]{3,0,2,1:T(8,128)(2,1)}, u32[]{:S(2)}) copy-start(bf16[256,16,1,256]{3,0,2,1:T(8,128)(2,1)} %get-tuple-element.46) | copy-start | bytes 6291460
  272.1 8.4 %copy-start.12 = (bf16[256,128]{1,0:T(8,128)(2,1)S(1)}, bf16[256,128]{1,0:T(8,128)(2,1)}, u32[]{:S(2)}) copy-start(bf16[256,128]{1,0:T(8,128)(2,1)} %all-reduce.2.cloned.1.call-done) | copy-start | bytes 196612
  280.5 71.8 %reduce-scatter.11.cloned.1.call-start = ((), (), s32[]{:S(2)}) async-start(), calls=%async_computation.10 | async-start | bytes 1310720 | tf_op jit(solution)/shard_map/reduce_scatter | solution.py:131
  282.1 157.8 %reduce-scatter.5.cloned.1.call-start = ((), (), s32[]{:S(2)}) async-start(), calls=%async_computation.7 | async-start | bytes 7864320 | tf_op jit(solution)/shard_map/reduce_scatter | solution.py:98
  282.3 1.6 copy-start.9
  282.3 2.2 copy-start.10
  299.8 253.5 %reduce-scatter.7.cloned.1.call-start = ((), (), s32[]{:S(2)}) async-start(), calls=%async_computation.8 | async-start | bytes 7864320 | tf_op jit(solution)/shard_map/reduce_scatter | solution.py:109
  299.9 2.4 copy-start.7
  299.9 2.9 copy-start.8
  323.5 25.8 %collective-permute-start.3 = (bf16[256,2048]{1,0:T(8,128)(2,1)}, bf16[256,2048]{1,0:T(8,128)(2,1)}, u32[]{:S(2)}, u32[]{:S(2)}) collective-permute-start(bf16[256,2048]{1,0:T(8,128)(2,1)} %bitcast.64), channel_id=1, source_target_pairs={{0,2},{2,0},{1,3},{3,1},{4,6},{6,4},{5,7},{7,5},{8,10},{10,8},{9,1... | collective-permute-start | bytes 3145736 | tf_op jit(solution)/shard_map/ppermute | solution.py:18
  329.9 19.3 %collective-permute-start.2 = (bf16[256,2048]{1,0:T(8,128)(2,1)}, bf16[256,2048]{1,0:T(8,128)(2,1)}, u32[]{:S(2)}, u32[]{:S(2)}) collective-permute-start(bf16[256,2048]{1,0:T(8,128)(2,1)} %bitcast.62), channel_id=1, source_target_pairs={{0,1},{1,0},{2,3},{3,2},{4,5},{5,4},{6,7},{7,6},{8,9},{9,8},{10,11... | collective-permute-start | bytes 3145736 | tf_op jit(solution)/shard_map/ppermute | solution.py:18
  333.6 15.7 %copy-start.11 = (bf16[128,2048]{1,0:T(8,128)(2,1)S(1)}, bf16[128,2048]{1,0:T(8,128)(2,1)}, u32[]{:S(2)}) copy-start(bf16[128,2048]{1,0:T(8,128)(2,1)} %param.14) | copy-start | bytes 1572868
  439.9 117.0 %copy-start.1 = (bf16[128,4096]{1,0:T(8,128)(2,1)S(1)}, bf16[128,4096]{1,0:T(8,128)(2,1)}, u32[]{:S(2)}) copy-start(bf16[128,4096]{1,0:T(8,128)(2,1)} %param.15) | copy-start | bytes 3145732
Sparse Core Ops, SparseCore 0:
  11.4 118.0 all-gather.3
  131.1 113.5 all-gather.5
  280.6 20.0 reduce-scatter.8
  302.8 25.5 reduce-scatter.10
  330.5 109.3 reduce-scatter.4
  442.0 111.2 reduce-scatter.6
Sparse Core Ops, SparseCore 1:
  20.4 31.8 all-reduce.1
